TPU v7x, 256 devices: a whole 4x4x8 slice. The times are simulated.
256 devices in a mesh: row: 16 (over y, x), col: 16 (over z, core).
Axes of the slice: x: 4, y: 4, z: 8, core: 2. Of those that a mesh axis runs over, the one named last changes fastest.
Arguments:
- probe_block: bfloat16 [64, 262144], P(None, ('row', 'col'))
- prior_blocks: bfloat16 [4, 64, 262144], P(None, None, ('row', 'col'))
- self_relatedness: float32 [262144], P(('row', 'col')), may hold values from 0.5 to 2
- tile_values: bfloat16 [1280, 1024, 1024], P(('row', 'col')), may hold values from -0.125 to 0.125
- tile_index: int32 [1280, 3], P(('row', 'col')), may hold values from 0 to 255, as said below
Outputs:
- residual_block: float32 [64, 262144], P(None, ('row', 'col'))
- coefficients: float32 [5, 64, 64], replicated
Inputs may be any that keep to these rules, and one draw needn't show every extreme that they name: `tile_index`: rows d * 5 to d * 5 + 4 belong to the device d = r * C + c at mesh position (r, c), C the size of the col axis. In a row with column 2 equal to 1 (live) the tile row lies in [r * C, r * C + C), the tile column j has j % C == c, and tile row <= tile column; live pairs of one device are distinct. Column 2 is 0 in dead rows, which repeat the indices of the device's first row. Live counts vary between devices (not all equal), and some device has all 5 rows live.
All inputs are finite; a program needn't handle non-finite values.
Results may differ from a plain program's by a relative error of at most 0.0003.
Values may be sent and summed in bfloat16 or wider, within the bound.
No kernel may reach another device: no remote copies, remote signals or barrier semaphores. Data moves between devices by JAX's collectives and lax.ppermute only.
A program may use at most 128 MiB of HBM per device.

v0:
```python
import jax
import jax.numpy as jnp
from jax import lax
from jax.sharding import PartitionSpec as P


def add_span(running, addend, offset):
    current = lax.dynamic_slice_in_dim(running, offset, addend.shape[1], 1)
    return lax.dynamic_update_slice_in_dim(running, current + addend, offset, 1)


def keep_same(partials):
    return partials


def tile_products(tile_values, tile_index, row_probes, col_probes, col_count):
    tile_width = tile_values.shape[1]
    depth = row_probes.shape[0]
    partials = []
    partials.append(jnp.zeros((depth, row_probes.shape[1]), jnp.float32))
    partials.append(jnp.zeros((depth, col_probes.shape[1]), jnp.float32))
    partials = tuple(partials)
    for slot_index in range(tile_values.shape[0]):
        current_tile = tile_values[slot_index]
        row_start = tile_index[slot_index, 0] % col_count * tile_width
        col_start = tile_index[slot_index, 1] // col_count * tile_width

        def apply(state, current_tile=current_tile, row_start=row_start, col_start=col_start):
            updated = list(state)
            position = 0
            right = lax.dynamic_slice_in_dim(col_probes, col_start, tile_width, 1)
            forward = lax.dot_general(
                right, current_tile, (((1,), (1,)), ((), ())), preferred_element_type=jnp.float32
            )
            updated[0] = add_span(updated[0], forward, row_start)
            position = 1
            left = lax.dynamic_slice_in_dim(row_probes, row_start, tile_width, 1)
            mirror = jnp.dot(left, current_tile, preferred_element_type=jnp.float32)
            updated[position] = add_span(updated[position], mirror, col_start)
            return tuple(updated)

        partials = lax.cond(tile_index[slot_index, 2] > 0, apply, keep_same, partials)
    return partials


def sum_rows(row_part):
    return lax.psum_scatter(row_part, "col", scatter_dimension=1, tiled=True)


def sum_columns(col_part):
    return lax.psum_scatter(col_part, "row", scatter_dimension=1, tiled=True)


def solve_block(gram_block, target):
    factor = jnp.linalg.cholesky(gram_block)
    return jax.scipy.linalg.cho_solve((factor, True), target)


def shards(probe_block, prior_blocks, self_relatedness, tile_values, tile_index):
    col_count = lax.axis_size("col")
    block_count = prior_blocks.shape[0] + 1
    basis = jnp.concatenate([prior_blocks, probe_block[None]], axis=0)
    row_probes = lax.all_gather(probe_block, "col", axis=1, tiled=True)
    col_probes = lax.all_gather(probe_block, "row", axis=1, tiled=True)
    row_part, col_part = tile_products(tile_values, tile_index, row_probes, col_probes, col_count)
    row_total = sum_rows(row_part)
    col_total = sum_columns(col_part)
    product = self_relatedness[None, :] * probe_block.astype(jnp.float32) + row_total + col_total
    current = product
    solved = []
    for block_number in range(block_count):
        basis_block = basis[block_number]
        wide_block = basis_block.astype(jnp.float32)
        gram_local = jnp.dot(basis_block, basis_block.T, preferred_element_type=jnp.float32)
        along_local = jnp.dot(wide_block, current.T, precision=lax.Precision.HIGHEST)
        gram_block, along = lax.psum((gram_local, along_local), ("row", "col"))
        coefficient = solve_block(gram_block, along)
        solved.append(coefficient)
        current = current - jnp.dot(coefficient.T, wide_block, precision=lax.Precision.HIGHEST)
    return (current, jnp.stack(solved))


def solution(mesh):
    in_specs = (
        P(None, ("row", "col")),
        P(None, None, ("row", "col")),
        P(("row", "col")),
        P(("row", "col"), None, None),
        P(("row", "col"), None),
    )
    out_specs = (P(None, ("row", "col")), P())
    return jax.shard_map(shards, mesh=mesh, in_specs=in_specs, out_specs=out_specs, check_vma=False)
```

profile of v0, /device:TPU:8, one launch (start us, length us, event | category | flops | bytes accessed | tf_op | source)
XLA Modules:
  0.0 744.8 jit_solution(3812863163421222120)
XLA Ops:
  7.2 0.7 all-gather.3.cloned.1.call-update
  7.9 0.7 all-gather.5.cloned.1.call-update
  8.7 1.9 fusion.98
  31.8 5.8 slice_bitcast_fusion
  37.6 25.4 %all-gather.3.cloned.1.call-done = bf16[64,16384]{1,0:T(8,128)(2,1)} async-done(((bf16[64,1024]{1,0:T(8,128)(2,1)}), bf16[64,16384]{1,0:T(8,128)(2,1)}) %all-gather.3.cloned.1.call-update) | async-done | bytes 2097168 | tf_op jit(solution)/shard_map/all_gather | solution.py:64
  63.0 41.4 %all-gather.5.cloned.1.call-done = bf16[64,16384]{1,0:T(8,128)(2,1)} async-done(((bf16[64,1024]{1,0:T(8,128)(2,1)}), bf16[64,16384]{1,0:T(8,128)(2,1)}) %all-gather.5.cloned.1.call-update) | async-done | bytes 2097168 | tf_op jit(solution)/shard_map/all_gather | solution.py:63
  104.4 12.6 %conditional.5 = (f32[64,16384]{1,0:T(8,128)}, f32[64,16384]{1,0:T(8,128)}) conditional(s32[]{:T(128)} %bitcast.6, () %tuple.49, (s32[]{:T(128)}, bf16[64,16384]{1,0:T(8,128)(2,1)}, bf16[1024,1024]{1,0:T(8,128)(2,1)}, s32[]{:T(128)}, bf16[64,16384]{1,0:T(8,128)(2,1)}) %tuple.50), branch_computations={%region_0.1_spmd, %region_1.2_spmd} | conditional | flops 268435456 | bytes 14418028 | solution.py:42
  104.4 2.4 fusion.2
  106.8 2.3 broadcast.64.clone
  109.1 1.7 dynamic_update_slice.26
  110.7 2.2 fusion
  112.9 2.3 broadcast.64.clone.1
  115.3 1.8 dynamic_update_slice.27
  117.0 8.2 %conditional.6 = ((f32[64,16384]{1,0:T(8,128)}, f32[64,16384]{1,0:T(8,128)})) conditional(s32[]{:T(128)} %bitcast.5, (f32[64,16384]{1,0:T(8,128)}, f32[64,16384]{1,0:T(8,128)}) %conditional.5, (s32[]{:T(128)}, f32[64,16384]{1,0:T(8,128)}, s32[]{:T(128)}, bf16[64,16384]{1,0:T(8,128)(2,1)}, bf16[1024,1024]{1,0:T(8,128)(2,1)}, ...), branch_computations={%region_2.3_spmd, %region_3.4_spmd} | conditional | flops 268566528 | bytes 6553716 | solution.py:42
  117.0 2.2 convolution_add_fusion
  119.2 1.8 dynamic_update_slice.29
  121.0 2.4 convolution_add_fusion.1
  123.4 1.8 dynamic_update_slice.28
  125.2 8.3 %conditional.7 = ((f32[64,16384]{1,0:T(8,128)}, f32[64,16384]{1,0:T(8,128)})) conditional(s32[]{:T(128)} %bitcast.4, (f32[64,16384]{1,0:T(8,128)}, f32[64,16384]{1,0:T(8,128)}) %get-tuple-element.388, (s32[]{:T(128)}, f32[64,16384]{1,0:T(8,128)}, s32[]{:T(128)}, bf16[64,16384]{1,0:T(8,128)(2,1)}, bf16[1024,1024]{1,0:T(8,128)(2,1)}, ...), branch_computations={%region_4.5_spmd, %region_5.6_spmd} | conditional | flops 268566528 | bytes 6553716 | solution.py:42
  125.2 2.2 convolution_add_fusion.2
  127.4 1.8 dynamic_update_slice.31
  129.3 2.4 convolution_add_fusion.3
  131.7 1.8 dynamic_update_slice.30
  133.5 7.0 conditional.8
  133.5 1.6 convolution_add_fusion.4
  135.1 1.8 dynamic_update_slice.33
  136.9 1.8 convolution_add_fusion.5
  138.7 1.8 dynamic_update_slice.32
  140.6 0.5 reduce-scatter.5.cloned.1.call-update
  141.1 0.5 copy-done.1
  142.5 70.9 %reduce-scatter.3.cloned.1.call-done = f32[64,1024]{1,0:T(8,128)} async-done(((f32[64,16384]{1,0:T(8,128)}), f32[64,1024]{1,0:T(8,128)}) %reduce-scatter.3.cloned.1.call-update) | async-done | bytes 262160 | tf_op jit(solution)/shard_map/reduce_scatter | solution.py:47
  213.4 84.2 %reduce-scatter.5.cloned.1.call-done = f32[64,1024]{1,0:T(8,128)} async-done(((f32[64,16384]{1,0:T(8,128)}), f32[64,1024]{1,0:T(8,128)}) %reduce-scatter.5.cloned.1.call-update) | async-done | bytes 262160 | tf_op jit(solution)/shard_map/reduce_scatter | solution.py:51
  297.7 1.3 convolution_bitcast_fusion.4
  299.0 74.3 %all-reduce.4 = (f32[64,64]{0,1:T(8,128)S(1)}, f32[64,64]{0,1:T(8,128)S(1)}) all-reduce(f32[64,64]{0,1:T(8,128)S(1)} %convolution_bitcast_fusion.4, f32[64,64]{0,1:T(8,128)S(1)} %fusion.54), channel_id=1, replica_groups=mesh['row'=16,'col'=16] {'row','col'}, use_global_device_ids=true, to_apply=%region_15.17 | all-reduce | flops 8192 | bytes 65536 | tf_op jit(solution)/shard_map/psum | solution.py:76
  373.4 5.8 cholesky.89
  379.3 0.6 compare_reduce_fusion.4
  379.9 0.7 fusion.68
  380.6 4.9 custom-call.11
  385.5 0.2 fusion.95
  385.9 1.3 convolution_subtract_fusion.4
  387.5 75.0 %all-reduce.3 = (f32[64,64]{0,1:T(8,128)S(1)}, f32[64,64]{0,1:T(8,128)S(1)}) all-reduce(f32[64,64]{0,1:T(8,128)S(1)} %convolution_bitcast_fusion.3, f32[64,64]{0,1:T(8,128)S(1)} %fusion.50), channel_id=1, replica_groups=mesh['row'=16,'col'=16] {'row','col'}, use_global_device_ids=true, to_apply=%region_17.20 | all-reduce | flops 8192 | bytes 65536 | tf_op jit(solution)/shard_map/psum | solution.py:76
  462.6 5.8 cholesky.100
  468.5 0.6 compare_reduce_fusion.3
  469.1 0.7 fusion.69
  469.8 4.9 custom-call.12
  475.1 0.3 convolution_subtract_fusion.3
  475.7 73.9 %all-reduce.2 = (f32[64,64]{0,1:T(8,128)S(1)}, f32[64,64]{0,1:T(8,128)S(1)}) all-reduce(f32[64,64]{0,1:T(8,128)S(1)} %convolution_bitcast_fusion.2, f32[64,64]{0,1:T(8,128)S(1)} %fusion.46), channel_id=1, replica_groups=mesh['row'=16,'col'=16] {'row','col'}, use_global_device_ids=true, to_apply=%region_19.22 | all-reduce | flops 8192 | bytes 65536 | tf_op jit(solution)/shard_map/psum | solution.py:76
  549.7 5.8 cholesky.111
  555.6 0.6 compare_reduce_fusion.2
  556.2 0.7 fusion.70
  556.9 4.9 custom-call.13
  562.2 0.3 convolution_subtract_fusion.2
  562.8 74.8 %all-reduce.1 = (f32[64,64]{0,1:T(8,128)S(1)}, f32[64,64]{0,1:T(8,128)S(1)}) all-reduce(f32[64,64]{0,1:T(8,128)S(1)} %convolution_bitcast_fusion.1, f32[64,64]{0,1:T(8,128)S(1)} %fusion.42), channel_id=1, replica_groups=mesh['row'=16,'col'=16] {'row','col'}, use_global_device_ids=true, to_apply=%region_21.24 | all-reduce | flops 8192 | bytes 65536 | tf_op jit(solution)/shard_map/psum | solution.py:76
  637.7 5.8 cholesky.122
  643.6 0.6 compare_reduce_fusion.1
  644.2 0.7 fusion.71
  644.9 4.9 custom-call.14
  650.2 0.3 convolution_subtract_fusion.1
  650.8 73.9 %all-reduce = (f32[64,64]{0,1:T(8,128)S(1)}, f32[64,64]{0,1:T(8,128)S(1)}) all-reduce(f32[64,64]{0,1:T(8,128)S(1)} %convolution_bitcast_fusion, f32[64,64]{0,1:T(8,128)S(1)} %fusion.99), channel_id=1, replica_groups=mesh['row'=16,'col'=16] {'row','col'}, use_global_device_ids=true, to_apply=%region_23.26 | all-reduce | flops 8192 | bytes 65536 | tf_op jit(solution)/shard_map/psum | solution.py:76
  724.7 5.8 cholesky.133
  730.6 0.6 compare_reduce_fusion
  731.2 0.7 fusion.72
  731.9 4.9 custom-call.15
  737.2 1.0 convolution_subtract_fusion
  (46 shorter events, 4.4 us)
Async XLA Ops:
  7.2 55.8 %all-gather.3.cloned.1.call-start = ((), (), s32[]{:S(2)}) async-start(), calls=%async_computation.2 | async-start | bytes 2228224 | tf_op jit(solution)/shard_map/all_gather | solution.py:64
  7.9 96.5 %all-gather.5.cloned.1.call-start = ((), (), s32[]{:S(2)}) async-start(), calls=%async_computation.3 | async-start | bytes 2228224 | tf_op jit(solution)/shard_map/all_gather | solution.py:63
  8.6 204.8 %reduce-scatter.3.cloned.1.call-start = ((), (), s32[]{:S(2)}) async-start(), calls=%async_computation.4 | async-start | bytes 4456448 | tf_op jit(solution)/shard_map/reduce_scatter | solution.py:47
  140.5 157.1 %reduce-scatter.5.cloned.1.call-start = ((), (), s32[]{:S(2)}) async-start(), calls=%async_computation.5 | async-start | bytes 4456448 | tf_op jit(solution)/shard_map/reduce_scatter | solution.py:51
  140.6 1.0 copy-start.1
  140.6 1.7 copy-start
  140.6 157.1 %copy-start.2 = (f32[1024]{0:T(1024)S(1)}, f32[1024]{0:T(1024)}, u32[]{:S(2)}) copy-start(f32[1024]{0:T(1024)} %param.20) | copy-start | bytes 12292
  737.2 1.0 copy-start.3
Sparse Core Ops, SparseCore 0:
  10.4 52.4 all-gather.2
  64.8 39.4 all-gather.4
  140.6 72.7 reduce-scatter.2
  216.9 80.7 reduce-scatter.4
where the time goes:
time: 747 us; the launch traced here: 745 us
  blocking collectives  372 us (50%)
  waiting for transfers between devices  224 us (30%)
  other arithmetic  60.4 us (8%)
  between operations  35.3 us (5%)
  local copies, waits for them, and re-layouts  27.4 us (4%)
  matrix products  25.8 us (3%)
    psum x5, blocking collectives, shards(): gram_block, along = lax.psum((gram_local, along_local), ('row', 'col'))  372 us
    reduce_scatter x1, waiting for transfers between devices, sum_columns(): return lax.psum_scatter(col_part, 'row', scatter_dimension=1, tiled=True)  84.2 us
    reduce_scatter x1, waiting for transfers between devices, sum_rows(): return lax.psum_scatter(row_part, 'col', scatter_dimension=1, tiled=True)  70.9 us
    all_gather x1, waiting for transfers between devices, shards(): row_probes = lax.all_gather(probe_block, 'col', axis=1, tiled=True)  41.4 us
    another operation x15, other arithmetic, solve_block(): factor = jnp.linalg.cholesky(gram_block)  32.6 us
    another operation x10, other arithmetic, solve_block(): return jax.scipy.linalg.cho_solve((factor, True), target)  27.7 us
    all_gather x1, waiting for transfers between devices, shards(): col_probes = lax.all_gather(probe_block, 'row', axis=1, tiled=True)  25.4 us
  transfers between devices with their start and end apart: 4, of which 4 were waited for; matrix products, arithmetic and copies ran while one was open for 1% of the time, Pallas kernels for 0%

commit v1 on v0

--- a/solution.py
+++ b/solution.py
@@ -27,16 +27,14 @@
 
         def apply(state, current_tile=current_tile, row_start=row_start, col_start=col_start):
             updated = list(state)
-            position = 0
             right = lax.dynamic_slice_in_dim(col_probes, col_start, tile_width, 1)
             forward = lax.dot_general(
                 right, current_tile, (((1,), (1,)), ((), ())), preferred_element_type=jnp.float32
             )
             updated[0] = add_span(updated[0], forward, row_start)
-            position = 1
             left = lax.dynamic_slice_in_dim(row_probes, row_start, tile_width, 1)
             mirror = jnp.dot(left, current_tile, preferred_element_type=jnp.float32)
-            updated[position] = add_span(updated[position], mirror, col_start)
+            updated[1] = add_span(updated[1], mirror, col_start)
             return tuple(updated)
 
         partials = lax.cond(tile_index[slot_index, 2] > 0, apply, keep_same, partials)
@@ -59,24 +57,29 @@
 def shards(probe_block, prior_blocks, self_relatedness, tile_values, tile_index):
     col_count = lax.axis_size("col")
     block_count = prior_blocks.shape[0] + 1
+    depth = probe_block.shape[0]
     basis = jnp.concatenate([prior_blocks, probe_block[None]], axis=0)
+    flat_basis = basis.reshape(block_count * depth, basis.shape[2])
+    wide_basis = flat_basis.astype(jnp.float32)
     row_probes = lax.all_gather(probe_block, "col", axis=1, tiled=True)
     col_probes = lax.all_gather(probe_block, "row", axis=1, tiled=True)
     row_part, col_part = tile_products(tile_values, tile_index, row_probes, col_probes, col_count)
     row_total = sum_rows(row_part)
     col_total = sum_columns(col_part)
     product = self_relatedness[None, :] * probe_block.astype(jnp.float32) + row_total + col_total
-    current = product
+    gram_local = jnp.dot(flat_basis, flat_basis.T, preferred_element_type=jnp.float32)
+    along_local = jnp.dot(wide_basis, product.T, precision=lax.Precision.HIGHEST)
+    gram, along = lax.psum((gram_local, along_local), ("row", "col"))
     solved = []
     for block_number in range(block_count):
-        basis_block = basis[block_number]
-        wide_block = basis_block.astype(jnp.float32)
-        gram_local = jnp.dot(basis_block, basis_block.T, preferred_element_type=jnp.float32)
-        along_local = jnp.dot(wide_block, current.T, precision=lax.Precision.HIGHEST)
-        gram_block, along = lax.psum((gram_local, along_local), ("row", "col"))
-        coefficient = solve_block(gram_block, along)
-        solved.append(coefficient)
-        current = current - jnp.dot(coefficient.T, wide_block, precision=lax.Precision.HIGHEST)
+        rows = slice(block_number * depth, (block_number + 1) * depth)
+        target = along[rows]
+        for earlier in range(block_number):
+            cross = gram[rows, earlier * depth:(earlier + 1) * depth]
+            target = target - jnp.dot(cross, solved[earlier], precision=lax.Precision.HIGHEST)
+        solved.append(solve_block(gram[rows, rows], target))
+    coefficients = jnp.concatenate(solved, axis=0)
+    current = product - jnp.dot(coefficients.T, wide_basis, precision=lax.Precision.HIGHEST)
     return (current, jnp.stack(solved))
 
 

time: 747 us -> 641 us (0.86)
  blocking collectives: 372 us -> 0 us
  waiting for transfers between devices: 224 us -> 485 us
    psum x5 -> x0, blocking collectives: 372 us -> none  [shards(): gram_block, along = lax.psum((gram_local, along_local), ('row', 'col'))]
    psum x0 -> x1, waiting for transfers between devices: none -> 254 us  [shards(): gram, along = lax.psum((gram_local, along_local), ('row', 'col'))]
    dot_general x15 -> x13, matrix products: 6.46 us -> 14.5 us  [the longest x10 9.58 us: shards(): jnp.dot(cross, solved[earlier], precision=lax.Precision.HIGHEST)]
  transfers between devices with their start and end apart: 4 -> 5, of which waited for: 4 -> 5; matrix products, arithmetic and copies ran while one was open for 1% -> 1% of each run, Pallas kernels for 0% -> 0%
where the time goes in v1:
time: 641 us; the launch traced here: 639 us
  waiting for transfers between devices  485 us (76%)
  other arithmetic  61.4 us (10%)
  between operations  35 us (5%)
  matrix products  31.6 us (5%)
  local copies, waits for them, and re-layouts  25.9 us (4%)
    psum x1, waiting for transfers between devices, shards(): gram, along = lax.psum((gram_local, along_local), ('row', 'col'))  254 us
    reduce_scatter x1, waiting for transfers between devices, sum_columns(): return lax.psum_scatter(col_part, 'row', scatter_dimension=1, tiled=True)  84.5 us
    reduce_scatter x1, waiting for transfers between devices, sum_rows(): return lax.psum_scatter(row_part, 'col', scatter_dimension=1, tiled=True)  76.8 us
    all_gather x1, waiting for transfers between devices, shards(): row_probes = lax.all_gather(probe_block, 'col', axis=1, tiled=True)  41.4 us
    another operation x15, other arithmetic, solve_block(): factor = jnp.linalg.cholesky(gram_block)  32.6 us
    another operation x10, other arithmetic, solve_block(): return jax.scipy.linalg.cho_solve((factor, True), target)  27.7 us
    all_gather x1, waiting for transfers between devices, shards(): col_probes = lax.all_gather(probe_block, 'row', axis=1, tiled=True)  25.6 us
  transfers between devices with their start and end apart: 5, of which 5 were waited for; matrix products, arithmetic and copies ran while one was open for 1% of the time, Pallas kernels for 0%

profile of v1, /device:TPU:8, one launch (start us, length us, event | category | flops | bytes accessed | tf_op | source)
XLA Modules:
  0.0 639.0 jit_solution(5508760464213600865)
XLA Ops:
  7.2 0.7 all-gather.3.cloned.1.call-update
  7.9 0.7 all-gather.5.cloned.1.call-update
  8.7 1.9 fusion.83
  31.5 5.8 slice_bitcast_fusion
  37.4 25.6 %all-gather.3.cloned.1.call-done = bf16[64,16384]{1,0:T(8,128)(2,1)} async-done(((bf16[64,1024]{1,0:T(8,128)(2,1)}), bf16[64,16384]{1,0:T(8,128)(2,1)}) %all-gather.3.cloned.1.call-update) | async-done | bytes 2097168 | tf_op jit(solution)/shard_map/all_gather | solution.py:65
  63.0 41.4 %all-gather.5.cloned.1.call-done = bf16[64,16384]{1,0:T(8,128)(2,1)} async-done(((bf16[64,1024]{1,0:T(8,128)(2,1)}), bf16[64,16384]{1,0:T(8,128)(2,1)}) %all-gather.5.cloned.1.call-update) | async-done | bytes 2097168 | tf_op jit(solution)/shard_map/all_gather | solution.py:64
  104.4 12.9 %conditional.5 = (f32[64,16384]{1,0:T(8,128)}, f32[64,16384]{1,0:T(8,128)}) conditional(s32[]{:T(128)} %bitcast.6, () %tuple.49, (s32[]{:T(128)}, bf16[64,16384]{1,0:T(8,128)(2,1)}, bf16[1024,1024]{1,0:T(8,128)(2,1)}, s32[]{:T(128)}, bf16[64,16384]{1,0:T(8,128)(2,1)}) %tuple.50), branch_computations={%region_0.1_spmd, %region_1.2_spmd} | conditional | flops 268435456 | bytes 14418028 | solution.py:40
  104.4 2.4 fusion.2
  106.8 2.3 broadcast.64.clone
  109.1 1.8 dynamic_update_slice.26
  110.9 2.2 fusion
  113.1 2.3 broadcast.64.clone.1
  115.4 1.9 dynamic_update_slice.27
  117.3 8.3 %conditional.6 = ((f32[64,16384]{1,0:T(8,128)}, f32[64,16384]{1,0:T(8,128)})) conditional(s32[]{:T(128)} %bitcast.5, (f32[64,16384]{1,0:T(8,128)}, f32[64,16384]{1,0:T(8,128)}) %conditional.5, (s32[]{:T(128)}, f32[64,16384]{1,0:T(8,128)}, s32[]{:T(128)}, bf16[64,16384]{1,0:T(8,128)(2,1)}, bf16[1024,1024]{1,0:T(8,128)(2,1)}, ...), branch_computations={%region_2.3_spmd, %region_3.4_spmd} | conditional | flops 268566528 | bytes 6553716 | solution.py:40
  117.3 2.2 convolution_add_fusion
  119.5 1.8 dynamic_update_slice.29
  121.4 2.4 convolution_add_fusion.1
  123.8 1.8 dynamic_update_slice.28
  125.6 8.3 %conditional.7 = ((f32[64,16384]{1,0:T(8,128)}, f32[64,16384]{1,0:T(8,128)})) conditional(s32[]{:T(128)} %bitcast.4, (f32[64,16384]{1,0:T(8,128)}, f32[64,16384]{1,0:T(8,128)}) %get-tuple-element.394, (s32[]{:T(128)}, f32[64,16384]{1,0:T(8,128)}, s32[]{:T(128)}, bf16[64,16384]{1,0:T(8,128)(2,1)}, bf16[1024,1024]{1,0:T(8,128)(2,1)}, ...), branch_computations={%region_4.5_spmd, %region_5.6_spmd} | conditional | flops 268566528 | bytes 6553716 | solution.py:40
  125.6 2.2 convolution_add_fusion.2
  127.8 1.8 dynamic_update_slice.31
  129.7 2.4 convolution_add_fusion.3
  132.1 1.8 dynamic_update_slice.30
  134.1 0.5 reduce-scatter.5.cloned.1.call-update
  135.2 1.4 fusion.84
  136.6 76.8 %reduce-scatter.3.cloned.1.call-done = f32[64,1024]{1,0:T(8,128)} async-done(((f32[64,16384]{1,0:T(8,128)}), f32[64,1024]{1,0:T(8,128)}) %reduce-scatter.3.cloned.1.call-update) | async-done | bytes 262160 | tf_op jit(solution)/shard_map/reduce_scatter | solution.py:45
  213.4 84.5 %reduce-scatter.5.cloned.1.call-done = f32[64,1024]{1,0:T(8,128)} async-done(((f32[64,16384]{1,0:T(8,128)}), f32[64,1024]{1,0:T(8,128)}) %reduce-scatter.5.cloned.1.call-update) | async-done | bytes 262160 | tf_op jit(solution)/shard_map/reduce_scatter | solution.py:49
  297.9 2.4 fusion.81
  300.3 254.4 %all-reduce.3.cloned.1.call-done = (f32[320,64]{0,1:T(8,128)}, f32[320,320]{0,1:T(8,128)}) async-done(((f32[320,64]{0,1:T(8,128)}, f32[320,320]{0,1:T(8,128)}), (f32[320,64]{0,1:T(8,128)}, f32[320,320]{0,1:T(8,128)})) %all-reduce.3.cloned.1.call-update) | async-done | bytes 491536 | tf_op jit(solution)/shard_map/psum | solution.py:72
  554.7 0.9 fusion.82
  556.0 1.0 fusion.61
  557.0 5.8 cholesky.89
  562.9 0.6 compare_reduce_fusion.4
  563.5 0.7 fusion.40
  564.2 4.9 custom-call.11
  569.1 1.0 fusion.55
  570.4 0.9 convolution_subtract_fusion.4
  571.3 1.0 convolution_subtract_fusion.10
  572.3 0.9 convolution_subtract_fusion.9
  573.3 1.0 convolution_subtract_fusion.7
  574.3 5.8 cholesky.133
  580.2 0.6 compare_reduce_fusion
  580.8 0.7 fusion.44
  581.5 4.9 custom-call.15
  586.4 5.9 cholesky.100
  592.3 0.6 compare_reduce_fusion.3
  592.9 0.7 fusion.41
  593.6 4.9 custom-call.12
  598.5 5.9 cholesky.111
  604.4 0.6 compare_reduce_fusion.2
  605.0 0.7 fusion.42
  605.7 4.9 custom-call.13
  611.1 0.9 convolution_subtract_fusion.3
  612.0 0.9 convolution_subtract_fusion.8
  612.9 5.8 cholesky.122
  618.8 0.6 compare_reduce_fusion.1
  619.4 0.7 fusion.43
  620.1 4.9 custom-call.14
  625.0 1.0 convolution_subtract_fusion.6
  626.5 0.9 convolution_subtract_fusion.2
  627.4 1.0 convolution_subtract_fusion.5
  628.9 0.9 convolution_subtract_fusion.1
  630.4 0.8 copy.13
  631.2 1.2 convolution_subtract_fusion
  (40 shorter events, 3.6 us)
Async XLA Ops:
  7.2 55.8 %all-gather.3.cloned.1.call-start = ((), (), s32[]{:S(2)}) async-start(), calls=%async_computation.2 | async-start | bytes 2228224 | tf_op jit(solution)/shard_map/all_gather | solution.py:65
  7.9 96.5 %all-gather.5.cloned.1.call-start = ((), (), s32[]{:S(2)}) async-start(), calls=%async_computation.3 | async-start | bytes 2228224 | tf_op jit(solution)/shard_map/all_gather | solution.py:64
  8.6 204.8 %reduce-scatter.3.cloned.1.call-start = ((), (), s32[]{:S(2)}) async-start(), calls=%async_computation.4 | async-start | bytes 4456448 | tf_op jit(solution)/shard_map/reduce_scatter | solution.py:45
  134.0 163.9 %reduce-scatter.5.cloned.1.call-start = ((), (), s32[]{:S(2)}) async-start(), calls=%async_computation.5 | async-start | bytes 4456448 | tf_op jit(solution)/shard_map/reduce_scatter | solution.py:49
  134.0 0.9 copy-start
  134.1 1.1 copy-start.3
  134.6 163.3 %copy-start.4 = (f32[1024]{0:T(1024)S(1)}, f32[1024]{0:T(1024)}, u32[]{:S(2)}) copy-start(f32[1024]{0:T(1024)} %param.20) | copy-start | bytes 12292
  134.6 420.1 %all-reduce.3.cloned.1.call-start = ((), (), s32[]{:S(2)}) async-start(), calls=%async_computation.6 | async-start | bytes 1179648 | tf_op jit(solution)/shard_map/psum | solution.py:72
  555.9 75.3 %copy-start.1 = (f32[64,1024]{1,0:T(8,128)S(1)}, f32[64,1024]{1,0:T(8,128)}, u32[]{:S(2)}) copy-start(f32[64,1024]{1,0:T(8,128)} %reduce-scatter.3.cloned.1.call-done) | copy-start | bytes 786436
  556.0 75.3 %copy-start.2 = (f32[64,1024]{1,0:T(8,128)S(1)}, f32[64,1024]{1,0:T(8,128)}, u32[]{:S(2)}) copy-start(f32[64,1024]{1,0:T(8,128)} %reduce-scatter.5.cloned.1.call-done) | copy-start | bytes 786436
Sparse Core Ops, SparseCore 0:
  10.4 52.5 all-gather.2
  64.8 39.4 all-gather.4
  134.1 79.2 reduce-scatter.2
  216.9 80.9 reduce-scatter.4
  304.8 249.8 all-reduce.2

commit v2 on v1

--- a/solution.py
+++ b/solution.py
@@ -49,37 +49,60 @@
     return lax.psum_scatter(col_part, "row", scatter_dimension=1, tiled=True)
 
 
-def solve_block(gram_block, target):
+def hypercube_sum(value, axes):
+    for axis in axes:
+        size = lax.axis_size(axis)
+        if size & (size - 1):
+            value = lax.psum(value, axis)
+            continue
+        stride = 1
+        while stride < size:
+            pairs = [(index, index ^ stride) for index in range(size)]
+            value = value + lax.ppermute(value, axis, pairs)
+            stride *= 2
+    return value
+
+
+def inverse_factor(gram_block):
     factor = jnp.linalg.cholesky(gram_block)
-    return jax.scipy.linalg.cho_solve((factor, True), target)
+    identity = jnp.eye(gram_block.shape[0], dtype=gram_block.dtype)
+    return jax.scipy.linalg.solve_triangular(factor, identity, lower=True)
 
 
 def shards(probe_block, prior_blocks, self_relatedness, tile_values, tile_index):
     col_count = lax.axis_size("col")
     block_count = prior_blocks.shape[0] + 1
     depth = probe_block.shape[0]
+    highest = lax.Precision.HIGHEST
     basis = jnp.concatenate([prior_blocks, probe_block[None]], axis=0)
     flat_basis = basis.reshape(block_count * depth, basis.shape[2])
     wide_basis = flat_basis.astype(jnp.float32)
+    gram_local = jnp.dot(flat_basis, flat_basis.T, preferred_element_type=jnp.float32)
+    pairs = [(b, e) for b in range(block_count) for e in range(b + 1)]
+    lower_local = jnp.stack(
+        [gram_local[b * depth:(b + 1) * depth, e * depth:(e + 1) * depth] for b, e in pairs]
+    )
+    lower = hypercube_sum(lower_local, ("col", "row"))
+    gram = {pair: lower[n] for n, pair in enumerate(pairs)}
+    inverses = [inverse_factor(gram[(b, b)]) for b in range(block_count)]
     row_probes = lax.all_gather(probe_block, "col", axis=1, tiled=True)
     col_probes = lax.all_gather(probe_block, "row", axis=1, tiled=True)
     row_part, col_part = tile_products(tile_values, tile_index, row_probes, col_probes, col_count)
     row_total = sum_rows(row_part)
     col_total = sum_columns(col_part)
     product = self_relatedness[None, :] * probe_block.astype(jnp.float32) + row_total + col_total
-    gram_local = jnp.dot(flat_basis, flat_basis.T, preferred_element_type=jnp.float32)
-    along_local = jnp.dot(wide_basis, product.T, precision=lax.Precision.HIGHEST)
-    gram, along = lax.psum((gram_local, along_local), ("row", "col"))
+    along_local = jnp.dot(wide_basis, product.T, precision=highest)
+    along = hypercube_sum(along_local, ("col", "row"))
     solved = []
     for block_number in range(block_count):
-        rows = slice(block_number * depth, (block_number + 1) * depth)
-        target = along[rows]
+        target = along[block_number * depth:(block_number + 1) * depth]
         for earlier in range(block_number):
-            cross = gram[rows, earlier * depth:(earlier + 1) * depth]
-            target = target - jnp.dot(cross, solved[earlier], precision=lax.Precision.HIGHEST)
-        solved.append(solve_block(gram[rows, rows], target))
+            target = target - jnp.dot(gram[(block_number, earlier)], solved[earlier], precision=highest)
+        inverse = inverses[block_number]
+        half = jnp.dot(inverse, target, precision=highest)
+        solved.append(jnp.dot(inverse.T, half, precision=highest))
     coefficients = jnp.concatenate(solved, axis=0)
-    current = product - jnp.dot(coefficients.T, wide_basis, precision=lax.Precision.HIGHEST)
+    current = product - jnp.dot(coefficients.T, wide_basis, precision=highest)
     return (current, jnp.stack(solved))
 
 

time: 641 us -> 403 us (0.63)
  waiting for transfers between devices: 485 us -> 215 us
  starting transfers between devices: 0.37 us -> 39 us
  matrix products: 31.6 us -> 22.5 us
    psum x1 -> x0, waiting for transfers between devices: 254 us -> none  [shards(): gram, along = lax.psum((gram_local, along_local), ('row', 'col'))]
    ppermute x0 -> x16, waiting for transfers between devices: none -> 146 us  [hypercube_sum(): value = value + lax.ppermute(value, axis, pairs)]
    reduce_scatter x1, waiting for transfers between devices: 84.5 us -> 0.02 us  [sum_columns(): return lax.psum_scatter(col_part, 'row', scatter_dimension=1, tiled=True)]
    reduce_scatter x1, waiting for transfers between devices: 76.8 us -> 0.02 us  [sum_rows(): return lax.psum_scatter(row_part, 'col', scatter_dimension=1, tiled=True)]
    ppermute x0 -> x16, starting transfers between devices: none -> 38.8 us  [hypercube_sum(): value = value + lax.ppermute(value, axis, pairs)]
    dot_general x12 -> x22, matrix products: 13.2 us -> 6.85 us  [the longest x1 1.75 us: shards(): along_local = jnp.dot(wide_basis, product.T, precision=highest)]
  transfers between devices with their start and end apart: 5 -> 20, of which waited for: 5 -> 17; matrix products, arithmetic and copies ran while one was open for 1% -> 18% of each run, Pallas kernels for 0% -> 0%
where the time goes in v2:
time: 403 us; the launch traced here: 399 us
  waiting for transfers between devices  215 us (53%)
  other arithmetic  61 us (15%)
  starting transfers between devices  39 us (10%)
  between operations  35.9 us (9%)
  local copies, waits for them, and re-layouts  25.8 us (6%)
  matrix products  22.5 us (6%)
    ppermute x16, waiting for transfers between devices, hypercube_sum(): value = value + lax.ppermute(value, axis, pairs)  146 us
    all_gather x1, waiting for transfers between devices, shards(): row_probes = lax.all_gather(probe_block, 'col', axis=1, tiled=True)  41.4 us
    ppermute x16, starting transfers between devices, hypercube_sum(): value = value + lax.ppermute(value, axis, pairs)  38.8 us
    another operation x15, other arithmetic, inverse_factor(): factor = jnp.linalg.cholesky(gram_block)  32.6 us
    another operation x10, other arithmetic, inverse_factor(): return jax.scipy.linalg.solve_triangular(factor, identity, lower=True)  27.7 us
    all_gather x1, waiting for transfers between devices, shards(): col_probes = lax.all_gather(probe_block, 'row', axis=1, tiled=True)  25 us
    dynamic_update_slice x6, local copies, waits for them, and re-layouts, add_span(): return lax.dynamic_update_slice_in_dim(running, current + addend, offset, 1)  11 us
  transfers between devices with their start and end apart: 20, of which 17 were waited for; matrix products, arithmetic and copies ran while one was open for 18% of the time, Pallas kernels for 0%

profile of v2, /device:TPU:8, one launch (start us, length us, event | category | flops | bytes accessed | tf_op | source)
XLA Modules:
  0.0 398.9 jit_solution(3728455737215444936)
XLA Ops:
  7.2 0.7 all-gather.3.cloned.1.call-update
  7.9 0.7 all-gather.5.cloned.1.call-update
  8.7 1.9 fusion.91
  32.1 5.8 %slice_bitcast_fusion = (bf16[1024,1024]{1,0:T(8,128)(2,1)S(1)}, bf16[1024,1024]{1,0:T(8,128)(2,1)}, bf16[1024,1024]{1,0:T(8,128)(2,1)}, bf16[1024,1024]{1,0:T(8,128)(2,1)}) fusion(bf16[5,1024,1024]{2,1,0:T(8,128)(2,1)} %param.21), kind=kLoop, calls=%fused_computation.38 | loop fusion | bytes 16777216 | tf_op jit(solution)/shard_map/squeeze | solution.py:24
  37.9 25.0 %all-gather.3.cloned.1.call-done = bf16[64,16384]{1,0:T(8,128)(2,1)} async-done(((bf16[64,1024]{1,0:T(8,128)(2,1)}), bf16[64,16384]{1,0:T(8,128)(2,1)}) %all-gather.3.cloned.1.call-update) | async-done | bytes 2097168 | tf_op jit(solution)/shard_map/all_gather | solution.py:89
  63.0 41.4 %all-gather.5.cloned.1.call-done = bf16[64,16384]{1,0:T(8,128)(2,1)} async-done(((bf16[64,1024]{1,0:T(8,128)(2,1)}), bf16[64,16384]{1,0:T(8,128)(2,1)}) %all-gather.5.cloned.1.call-update) | async-done | bytes 2097168 | tf_op jit(solution)/shard_map/all_gather | solution.py:88
  104.3 12.9 %conditional.5 = (f32[64,16384]{1,0:T(8,128)}, f32[64,16384]{1,0:T(8,128)}) conditional(s32[]{:T(128)} %bitcast.6, () %tuple.49, (s32[]{:T(128)}, bf16[64,16384]{1,0:T(8,128)(2,1)}, bf16[1024,1024]{1,0:T(8,128)(2,1)}, s32[]{:T(128)}, bf16[64,16384]{1,0:T(8,128)(2,1)}) %tuple.50), branch_computations={%region_0.1_spmd, %region_1.2_spmd} | conditional | flops 268435456 | bytes 14418028 | solution.py:40
  104.3 2.4 fusion.2
  106.8 2.3 broadcast.52.clone
  109.1 1.8 dynamic_update_slice.26
  110.9 2.2 fusion
  113.1 2.3 broadcast.52.clone.1
  115.4 1.8 dynamic_update_slice.27
  117.2 8.3 %conditional.6 = ((f32[64,16384]{1,0:T(8,128)}, f32[64,16384]{1,0:T(8,128)})) conditional(s32[]{:T(128)} %bitcast.5, (f32[64,16384]{1,0:T(8,128)}, f32[64,16384]{1,0:T(8,128)}) %conditional.5, (s32[]{:T(128)}, f32[64,16384]{1,0:T(8,128)}, s32[]{:T(128)}, bf16[64,16384]{1,0:T(8,128)(2,1)}, bf16[1024,1024]{1,0:T(8,128)(2,1)}, ...), branch_computations={%region_2.3_spmd, %region_3.4_spmd} | conditional | flops 268566528 | bytes 6553716 | solution.py:40
  117.2 2.2 convolution_add_fusion
  119.4 1.9 dynamic_update_slice.29
  121.3 2.4 convolution_add_fusion.1
  123.7 1.8 dynamic_update_slice.28
  125.6 8.3 %conditional.7 = ((f32[64,16384]{1,0:T(8,128)}, f32[64,16384]{1,0:T(8,128)})) conditional(s32[]{:T(128)} %bitcast.4, (f32[64,16384]{1,0:T(8,128)}, f32[64,16384]{1,0:T(8,128)}) %get-tuple-element.390, (s32[]{:T(128)}, f32[64,16384]{1,0:T(8,128)}, s32[]{:T(128)}, bf16[64,16384]{1,0:T(8,128)(2,1)}, bf16[1024,1024]{1,0:T(8,128)(2,1)}, ...), branch_computations={%region_4.5_spmd, %region_5.6_spmd} | conditional | flops 268566528 | bytes 6553716 | solution.py:40
  125.6 2.2 convolution_add_fusion.2
  127.8 1.8 dynamic_update_slice.31
  129.6 2.4 convolution_add_fusion.3
  132.1 1.8 dynamic_update_slice.30
  136.3 1.9 collective-permute-done
  138.3 0.7 collective-permute-start.1
  139.0 12.7 %collective-permute-done.1 = f32[15,64,64]{1,2,0:T(8,128)S(1)} collective-permute-done((f32[15,64,64]{1,2,0:T(8,128)S(1)}, f32[15,64,64]{1,2,0:T(8,128)S(1)}, u32[]{:S(2)}, u32[]{:S(2)}) %collective-permute-start.1) | collective-permute-done | bytes 245792 | tf_op jit(solution)/shard_map/ppermute | solution.py:61
  151.7 1.6 collective-permute-start.2
  153.2 27.5 %collective-permute-done.2 = f32[15,64,64]{1,2,0:T(8,128)S(1)} collective-permute-done((f32[15,64,64]{1,2,0:T(8,128)S(1)}, f32[15,64,64]{1,2,0:T(8,128)S(1)}, u32[]{:S(2)}, u32[]{:S(2)}) %collective-permute-start.2) | collective-permute-done | bytes 245792 | tf_op jit(solution)/shard_map/ppermute | solution.py:61
  180.8 7.9 %collective-permute-start.3 = (f32[15,64,64]{1,2,0:T(8,128)S(1)}, f32[15,64,64]{1,2,0:T(8,128)S(1)}, u32[]{:S(2)}, u32[]{:S(2)}) collective-permute-start(f32[15,64,64]{1,2,0:T(8,128)S(1)} %add.188), channel_id=1, source_target_pairs={{0,8},{1,9},{2,10},{3,11},{4,12},{5,13},{6,14},{7,15},{8,0},{9,1},... | collective-permute-start | bytes 737288 | tf_op jit(solution)/shard_map/ppermute | solution.py:61
  188.7 24.5 %collective-permute-done.3 = f32[15,64,64]{1,2,0:T(8,128)S(1)} collective-permute-done((f32[15,64,64]{1,2,0:T(8,128)S(1)}, f32[15,64,64]{1,2,0:T(8,128)S(1)}, u32[]{:S(2)}, u32[]{:S(2)}) %collective-permute-start.3) | collective-permute-done | bytes 245792 | tf_op jit(solution)/shard_map/ppermute | solution.py:61
  213.3 6.8 %collective-permute-start.4 = (f32[15,64,64]{1,2,0:T(8,128)S(1)}, f32[15,64,64]{1,2,0:T(8,128)S(1)}, u32[]{:S(2)}, u32[]{:S(2)}) collective-permute-start(f32[15,64,64]{1,2,0:T(8,128)S(1)} %add.189), channel_id=1, source_target_pairs={{0,16},{16,0},{32,48},{48,32},{64,80},{80,64},{96,112},{112,96},{1... | collective-permute-start | bytes 737288 | tf_op jit(solution)/shard_map/ppermute | solution.py:61
  220.0 10.9 %collective-permute-done.4 = f32[15,64,64]{1,2,0:T(8,128)S(1)} collective-permute-done((f32[15,64,64]{1,2,0:T(8,128)S(1)}, f32[15,64,64]{1,2,0:T(8,128)S(1)}, u32[]{:S(2)}, u32[]{:S(2)}) %collective-permute-start.4) | collective-permute-done | bytes 245792 | tf_op jit(solution)/shard_map/ppermute | solution.py:61
  231.0 16.9 %collective-permute-start.5 = (f32[15,64,64]{1,2,0:T(8,128)S(1)}, f32[15,64,64]{1,2,0:T(8,128)S(1)}, u32[]{:S(2)}, u32[]{:S(2)}) collective-permute-start(f32[15,64,64]{1,2,0:T(8,128)S(1)} %add.190), channel_id=1, source_target_pairs={{0,32},{16,48},{32,0},{48,16},{64,96},{80,112},{96,64},{112,80},{1... | collective-permute-start | bytes 737288 | tf_op jit(solution)/shard_map/ppermute | solution.py:61
  247.9 13.0 %collective-permute-done.5 = f32[15,64,64]{1,2,0:T(8,128)S(1)} collective-permute-done((f32[15,64,64]{1,2,0:T(8,128)S(1)}, f32[15,64,64]{1,2,0:T(8,128)S(1)}, u32[]{:S(2)}, u32[]{:S(2)}) %collective-permute-start.5) | collective-permute-done | bytes 245792 | tf_op jit(solution)/shard_map/ppermute | solution.py:61
  261.0 1.4 collective-permute-start.6
  262.4 18.9 %collective-permute-done.6 = f32[15,64,64]{1,2,0:T(8,128)S(1)} collective-permute-done((f32[15,64,64]{1,2,0:T(8,128)S(1)}, f32[15,64,64]{1,2,0:T(8,128)S(1)}, u32[]{:S(2)}, u32[]{:S(2)}) %collective-permute-start.6) | collective-permute-done | bytes 245792 | tf_op jit(solution)/shard_map/ppermute | solution.py:61
  281.4 13.3 %collective-permute-done.7 = f32[15,64,64]{1,2,0:T(8,128)S(1)} collective-permute-done((f32[15,64,64]{1,2,0:T(8,128)S(1)}, f32[15,64,64]{1,2,0:T(8,128)S(1)}, u32[]{:S(2)}, u32[]{:S(2)}) %collective-permute-start.7) | collective-permute-done | bytes 245792 | tf_op jit(solution)/shard_map/ppermute | solution.py:61
  295.3 5.8 %cholesky.89 = f32[64,64]{1,0:T(8,128)S(1)} custom-call(f32[64,64]{1,0:T(8,128)S(1)} %get-tuple-element.337), custom_call_target="Cholesky" | custom-call | tf_op jit(solution)/shard_map/jit(cholesky)/cholesky | solution.py:67
  301.2 0.6 compare_reduce_fusion.4
  301.8 0.7 fusion.50
  302.5 4.9 %custom-call.9 = f32[1,64,64]{1,2,0:T(8,128)S(1)} custom-call(f32[1,64,64]{2,1,0:T(8,128)S(1)} %fusion.50), custom_call_target="InvertDiagBlocksLowerTriangular" | custom-call | tf_op jit(solution)/shard_map/jit(_solve_triangular)/triangular_solve | solution.py:69
  307.4 5.9 %cholesky.100 = f32[64,64]{1,0:T(8,128)S(1)} custom-call(f32[64,64]{1,0:T(8,128)S(1)} %get-tuple-element.338), custom_call_target="Cholesky" | custom-call | tf_op jit(solution)/shard_map/jit(cholesky)/cholesky | solution.py:67
  313.9 0.7 fusion.51
  314.6 4.9 %custom-call.10 = f32[1,64,64]{1,2,0:T(8,128)S(1)} custom-call(f32[1,64,64]{2,1,0:T(8,128)S(1)} %fusion.51), custom_call_target="InvertDiagBlocksLowerTriangular" | custom-call | tf_op jit(solution)/shard_map/jit(_solve_triangular)/triangular_solve | solution.py:69
  319.5 5.9 %cholesky.111 = f32[64,64]{1,0:T(8,128)S(1)} custom-call(f32[64,64]{1,0:T(8,128)S(1)} %get-tuple-element.339), custom_call_target="Cholesky" | custom-call | tf_op jit(solution)/shard_map/jit(cholesky)/cholesky | solution.py:67
  326.0 0.7 fusion.52
  326.7 4.9 %custom-call.11 = f32[1,64,64]{1,2,0:T(8,128)S(1)} custom-call(f32[1,64,64]{2,1,0:T(8,128)S(1)} %fusion.52), custom_call_target="InvertDiagBlocksLowerTriangular" | custom-call | tf_op jit(solution)/shard_map/jit(_solve_triangular)/triangular_solve | solution.py:69
  331.6 5.9 %cholesky.122 = f32[64,64]{1,0:T(8,128)S(1)} custom-call(f32[64,64]{1,0:T(8,128)S(1)} %get-tuple-element.340), custom_call_target="Cholesky" | custom-call | tf_op jit(solution)/shard_map/jit(cholesky)/cholesky | solution.py:67
  338.2 1.8 fusion.90
  340.1 1.3 collective-permute-done.8
  342.1 4.2 %collective-permute-done.9 = f32[320,64]{0,1:T(8,128)S(1)} collective-permute-done((f32[320,64]{0,1:T(8,128)S(1)}, f32[320,64]{0,1:T(8,128)S(1)}, u32[]{:S(2)}, u32[]{:S(2)}) %collective-permute-start.9) | collective-permute-done | bytes 81952 | tf_op jit(solution)/shard_map/ppermute | solution.py:61
  346.5 0.7 fusion.53
  347.1 4.9 %custom-call.12 = f32[1,64,64]{1,2,0:T(8,128)S(1)} custom-call(f32[1,64,64]{2,1,0:T(8,128)S(1)} %fusion.53), custom_call_target="InvertDiagBlocksLowerTriangular" | custom-call | tf_op jit(solution)/shard_map/jit(_solve_triangular)/triangular_solve | solution.py:69
  352.0 1.5 collective-permute-done.10
  354.1 5.8 %cholesky.133 = f32[64,64]{1,0:T(8,128)S(1)} custom-call(f32[64,64]{1,0:T(8,128)S(1)} %get-tuple-element.336), custom_call_target="Cholesky" | custom-call | tf_op jit(solution)/shard_map/jit(cholesky)/cholesky | solution.py:67
  359.9 3.4 collective-permute-done.11
  363.4 4.6 %collective-permute-done.12 = f32[320,64]{0,1:T(8,128)S(1)} collective-permute-done((f32[320,64]{0,1:T(8,128)S(1)}, f32[320,64]{0,1:T(8,128)S(1)}, u32[]{:S(2)}, u32[]{:S(2)}) %collective-permute-start.12) | collective-permute-done | bytes 81952 | tf_op jit(solution)/shard_map/ppermute | solution.py:61
  368.9 5.4 %collective-permute-done.13 = f32[320,64]{0,1:T(8,128)S(1)} collective-permute-done((f32[320,64]{0,1:T(8,128)S(1)}, f32[320,64]{0,1:T(8,128)S(1)}, u32[]{:S(2)}, u32[]{:S(2)}) %collective-permute-start.13) | collective-permute-done | bytes 81952 | tf_op jit(solution)/shard_map/ppermute | solution.py:61
  374.4 0.7 fusion.54
  375.1 4.9 %custom-call.13 = f32[1,64,64]{1,2,0:T(8,128)S(1)} custom-call(f32[1,64,64]{2,1,0:T(8,128)S(1)} %fusion.54), custom_call_target="InvertDiagBlocksLowerTriangular" | custom-call | tf_op jit(solution)/shard_map/jit(_solve_triangular)/triangular_solve | solution.py:69
  380.0 2.5 collective-permute-start.15
  382.8 3.5 collective-permute-done.15
  390.4 0.8 copy.27
  391.2 1.2 convolution_subtract_fusion
  (105 shorter events, 12.4 us)
Async XLA Ops:
  7.2 55.8 %all-gather.3.cloned.1.call-start = ((), (), s32[]{:S(2)}) async-start(), calls=%async_computation.2 | async-start | bytes 2228224 | tf_op jit(solution)/shard_map/all_gather | solution.py:89
  7.9 96.5 %all-gather.5.cloned.1.call-start = ((), (), s32[]{:S(2)}) async-start(), calls=%async_computation.3 | async-start | bytes 2228224 | tf_op jit(solution)/shard_map/all_gather | solution.py:88
  8.6 329.6 %reduce-scatter.3.cloned.1.call-start = ((), (), s32[]{:S(2)}) async-start(), calls=%async_computation.4 | async-start | bytes 4456448 | tf_op jit(solution)/shard_map/reduce_scatter | solution.py:45
  133.9 204.3 %reduce-scatter.5.cloned.1.call-start = ((), (), s32[]{:S(2)}) async-start(), calls=%async_computation.5 | async-start | bytes 4456448 | tf_op jit(solution)/shard_map/reduce_scatter | solution.py:49
  134.0 0.9 copy-start
  134.0 1.1 copy-start.3
  136.2 2.0 collective-permute-start
  138.3 13.4 %collective-permute-start.1 = (f32[15,64,64]{1,2,0:T(8,128)S(1)}, f32[15,64,64]{1,2,0:T(8,128)S(1)}, u32[]{:S(2)}, u32[]{:S(2)}) collective-permute-start(f32[15,64,64]{1,2,0:T(8,128)S(1)} %add.186), channel_id=1, source_target_pairs={{0,2},{1,3},{2,0},{3,1},{4,6},{5,7},{6,4},{7,5},{8,10},{9,11},{10,... | collective-permute-start | bytes 737288 | tf_op jit(solution)/shard_map/ppermute | solution.py:61
  151.7 29.1 %collective-permute-start.2 = (f32[15,64,64]{1,2,0:T(8,128)S(1)}, f32[15,64,64]{1,2,0:T(8,128)S(1)}, u32[]{:S(2)}, u32[]{:S(2)}) collective-permute-start(f32[15,64,64]{1,2,0:T(8,128)S(1)} %add.187), channel_id=1, source_target_pairs={{0,4},{1,5},{2,6},{3,7},{4,0},{5,1},{6,2},{7,3},{8,12},{9,13},{10,... | collective-permute-start | bytes 737288 | tf_op jit(solution)/shard_map/ppermute | solution.py:61
  180.8 32.4 %collective-permute-start.3 = (f32[15,64,64]{1,2,0:T(8,128)S(1)}, f32[15,64,64]{1,2,0:T(8,128)S(1)}, u32[]{:S(2)}, u32[]{:S(2)}) collective-permute-start(f32[15,64,64]{1,2,0:T(8,128)S(1)} %add.188), channel_id=1, source_target_pairs={{0,8},{1,9},{2,10},{3,11},{4,12},{5,13},{6,14},{7,15},{8,0},{9,1},... | collective-permute-start | bytes 737288 | tf_op jit(solution)/shard_map/ppermute | solution.py:61
  213.3 17.7 %collective-permute-start.4 = (f32[15,64,64]{1,2,0:T(8,128)S(1)}, f32[15,64,64]{1,2,0:T(8,128)S(1)}, u32[]{:S(2)}, u32[]{:S(2)}) collective-permute-start(f32[15,64,64]{1,2,0:T(8,128)S(1)} %add.189), channel_id=1, source_target_pairs={{0,16},{16,0},{32,48},{48,32},{64,80},{80,64},{96,112},{112,96},{1... | collective-permute-start | bytes 737288 | tf_op jit(solution)/shard_map/ppermute | solution.py:61
  231.0 29.9 %collective-permute-start.5 = (f32[15,64,64]{1,2,0:T(8,128)S(1)}, f32[15,64,64]{1,2,0:T(8,128)S(1)}, u32[]{:S(2)}, u32[]{:S(2)}) collective-permute-start(f32[15,64,64]{1,2,0:T(8,128)S(1)} %add.190), channel_id=1, source_target_pairs={{0,32},{16,48},{32,0},{48,16},{64,96},{80,112},{96,64},{112,80},{1... | collective-permute-start | bytes 737288 | tf_op jit(solution)/shard_map/ppermute | solution.py:61
  261.0 77.3 %copy-start.4 = (f32[1024]{0:T(1024)S(1)}, f32[1024]{0:T(1024)}, u32[]{:S(2)}) copy-start(f32[1024]{0:T(1024)} %param.20) | copy-start | bytes 12292
  261.0 20.3 %collective-permute-start.6 = (f32[15,64,64]{1,2,0:T(8,128)S(1)}, f32[15,64,64]{1,2,0:T(8,128)S(1)}, u32[]{:S(2)}, u32[]{:S(2)}) collective-permute-start(f32[15,64,64]{1,2,0:T(8,128)S(1)} %add.191), channel_id=1, source_target_pairs={{0,64},{16,80},{32,96},{48,112},{64,0},{80,16},{96,32},{112,48},{1... | collective-permute-start | bytes 737288 | tf_op jit(solution)/shard_map/ppermute | solution.py:61
  281.3 13.4 %collective-permute-start.7 = (f32[15,64,64]{1,2,0:T(8,128)S(1)}, f32[15,64,64]{1,2,0:T(8,128)S(1)}, u32[]{:S(2)}, u32[]{:S(2)}) collective-permute-start(f32[15,64,64]{1,2,0:T(8,128)S(1)} %add.192), channel_id=1, source_target_pairs={{0,128},{16,144},{32,160},{48,176},{64,192},{80,208},{96,224},{112... | collective-permute-start | bytes 737288 | tf_op jit(solution)/shard_map/ppermute | solution.py:61
  340.0 1.4 collective-permute-start.8
  341.4 4.9 %collective-permute-start.9 = (f32[320,64]{0,1:T(8,128)S(1)}, f32[320,64]{0,1:T(8,128)S(1)}, u32[]{:S(2)}, u32[]{:S(2)}) collective-permute-start(f32[320,64]{0,1:T(8,128)S(1)} %add.194), channel_id=1, source_target_pairs={{0,2},{1,3},{2,0},{3,1},{4,6},{5,7},{6,4},{7,5},{8,10},{9,11},{10,... | collective-permute-start | bytes 245768 | tf_op jit(solution)/shard_map/ppermute | solution.py:61
  346.4 7.1 %collective-permute-start.10 = (f32[320,64]{0,1:T(8,128)S(1)}, f32[320,64]{0,1:T(8,128)S(1)}, u32[]{:S(2)}, u32[]{:S(2)}) collective-permute-start(f32[320,64]{0,1:T(8,128)S(1)} %add.195), channel_id=1, source_target_pairs={{0,4},{1,5},{2,6},{3,7},{4,0},{5,1},{6,2},{7,3},{8,12},{9,13},{10,... | collective-permute-start | bytes 245768 | tf_op jit(solution)/shard_map/ppermute | solution.py:61
  353.5 9.8 %collective-permute-start.11 = (f32[320,64]{0,1:T(8,128)S(1)}, f32[320,64]{0,1:T(8,128)S(1)}, u32[]{:S(2)}, u32[]{:S(2)}) collective-permute-start(f32[320,64]{0,1:T(8,128)S(1)} %add.196), channel_id=1, source_target_pairs={{0,8},{1,9},{2,10},{3,11},{4,12},{5,13},{6,14},{7,15},{8,0},{9,1},... | collective-permute-start | bytes 245768 | tf_op jit(solution)/shard_map/ppermute | solution.py:61
  363.3 4.7 %collective-permute-start.12 = (f32[320,64]{0,1:T(8,128)S(1)}, f32[320,64]{0,1:T(8,128)S(1)}, u32[]{:S(2)}, u32[]{:S(2)}) collective-permute-start(f32[320,64]{0,1:T(8,128)S(1)} %add.197), channel_id=1, source_target_pairs={{0,16},{16,0},{32,48},{48,32},{64,80},{80,64},{96,112},{112,96},{1... | collective-permute-start | bytes 245768 | tf_op jit(solution)/shard_map/ppermute | solution.py:61
  368.1 23.1 %copy-start.1 = (f32[64,1024]{1,0:T(8,128)S(1)}, f32[64,1024]{1,0:T(8,128)}, u32[]{:S(2)}) copy-start(f32[64,1024]{1,0:T(8,128)} %reduce-scatter.3.cloned.1.call-done) | copy-start | bytes 786436
  368.1 23.1 %copy-start.2 = (f32[64,1024]{1,0:T(8,128)S(1)}, f32[64,1024]{1,0:T(8,128)}, u32[]{:S(2)}) copy-start(f32[64,1024]{1,0:T(8,128)} %reduce-scatter.5.cloned.1.call-done) | copy-start | bytes 786436
  368.1 6.2 %collective-permute-start.13 = (f32[320,64]{0,1:T(8,128)S(1)}, f32[320,64]{0,1:T(8,128)S(1)}, u32[]{:S(2)}, u32[]{:S(2)}) collective-permute-start(f32[320,64]{0,1:T(8,128)S(1)} %add.198), channel_id=1, source_target_pairs={{0,32},{16,48},{32,0},{48,16},{64,96},{80,112},{96,64},{112,80},{1... | collective-permute-start | bytes 245768 | tf_op jit(solution)/shard_map/ppermute | solution.py:61
  374.3 5.7 %collective-permute-start.14 = (f32[320,64]{0,1:T(8,128)S(1)}, f32[320,64]{0,1:T(8,128)S(1)}, u32[]{:S(2)}, u32[]{:S(2)}) collective-permute-start(f32[320,64]{0,1:T(8,128)S(1)} %add.199), channel_id=1, source_target_pairs={{0,64},{16,80},{32,96},{48,112},{64,0},{80,16},{96,32},{112,48},{1... | collective-permute-start | bytes 245768 | tf_op jit(solution)/shard_map/ppermute | solution.py:61
  380.0 6.2 %collective-permute-start.15 = (f32[320,64]{0,1:T(8,128)S(1)}, f32[320,64]{0,1:T(8,128)S(1)}, u32[]{:S(2)}, u32[]{:S(2)}) collective-permute-start(f32[320,64]{0,1:T(8,128)S(1)} %add.200), channel_id=1, source_target_pairs={{0,128},{16,144},{32,160},{48,176},{64,192},{80,208},{96,224},{112... | collective-permute-start | bytes 245768 | tf_op jit(solution)/shard_map/ppermute | solution.py:61
Sparse Core Ops, SparseCore 0:
  10.4 52.4 all-gather.2
  64.8 39.4 all-gather.4
  134.0 100.6 reduce-scatter.2
  238.2 86.8 reduce-scatter.4

commit v3 on v2

--- a/solution.py
+++ b/solution.py
@@ -83,13 +83,15 @@
         [gram_local[b * depth:(b + 1) * depth, e * depth:(e + 1) * depth] for b, e in pairs]
     )
     lower = hypercube_sum(lower_local, ("col", "row"))
+    row_probes = lax.all_gather(probe_block, "col", axis=1, tiled=True)
+    col_probes = lax.all_gather(probe_block, "row", axis=1, tiled=True)
+    lower, row_probes, col_probes = lax.optimization_barrier((lower, row_probes, col_probes))
     gram = {pair: lower[n] for n, pair in enumerate(pairs)}
     inverses = [inverse_factor(gram[(b, b)]) for b in range(block_count)]
-    row_probes = lax.all_gather(probe_block, "col", axis=1, tiled=True)
-    col_probes = lax.all_gather(probe_block, "row", axis=1, tiled=True)
     row_part, col_part = tile_products(tile_values, tile_index, row_probes, col_probes, col_count)
     row_total = sum_rows(row_part)
     col_total = sum_columns(col_part)
+    row_total, col_total, inverses = lax.optimization_barrier((row_total, col_total, inverses))
     product = self_relatedness[None, :] * probe_block.astype(jnp.float32) + row_total + col_total
     along_local = jnp.dot(wide_basis, product.T, precision=highest)
     along = hypercube_sum(along_local, ("col", "row"))

time: 403 us -> 412 us (1.022)
  waiting for transfers between devices: 215 us -> 251 us
  matrix products: 22.5 us -> 13.2 us
  local copies, waits for them, and re-layouts: 25.8 us -> 16.5 us
  starting transfers between devices: 39 us -> 33.2 us
    reduce_scatter x1, waiting for transfers between devices: 0.02 us -> 84.6 us  [sum_columns(): return lax.psum_scatter(col_part, 'row', scatter_dimension=1, tiled=True)]
    all_gather x1, waiting for transfers between devices: 41.4 us -> 0.02 us  [shards(): row_probes = lax.all_gather(probe_block, 'col', axis=1, tiled=True)]
    reduce_scatter x1, waiting for transfers between devices: 0.02 us -> 38 us  [sum_rows(): return lax.psum_scatter(row_part, 'col', scatter_dimension=1, tiled=True)]
    all_gather x1, waiting for transfers between devices: 25 us -> 0.02 us  [shards(): col_probes = lax.all_gather(probe_block, 'row', axis=1, tiled=True)]
    ppermute x16, waiting for transfers between devices: 146 us -> 126 us  [hypercube_sum(): value = value + lax.ppermute(value, axis, pairs)]
    dynamic_update_slice x6 -> x2, local copies, waits for them, and re-layouts: 11 us -> 3.6 us  [add_span(): return lax.dynamic_update_slice_in_dim(running, current + addend, offset, 1)]
    ppermute x16, starting transfers between devices: 38.8 us -> 32.8 us  [hypercube_sum(): value = value + lax.ppermute(value, axis, pairs)]
    dot_general x3 -> x1, matrix products: 7.31 us -> 2.44 us  [apply(): lax.dot_general(right, current_tile, (((1,), (1,)), ((), ())), preferred_...]
  transfers between devices with their start and end apart: 20 -> 20, of which waited for: 17 -> 17; matrix products, arithmetic and copies ran while one was open for 18% -> 17% of each run, Pallas kernels for 0% -> 0%
where the time goes in v3:
time: 412 us; the launch traced here: 411 us
  waiting for transfers between devices  251 us (61%)
  other arithmetic  62.2 us (15%)
  between operations  35.3 us (9%)
  starting transfers between devices  33.2 us (8%)
  local copies, waits for them, and re-layouts  16.5 us (4%)
  matrix products  13.2 us (3%)
    ppermute x16, waiting for transfers between devices, hypercube_sum(): value = value + lax.ppermute(value, axis, pairs)  126 us
    reduce_scatter x1, waiting for transfers between devices, sum_columns(): return lax.psum_scatter(col_part, 'row', scatter_dimension=1, tiled=True)  84.6 us
    reduce_scatter x1, waiting for transfers between devices, sum_rows(): return lax.psum_scatter(row_part, 'col', scatter_dimension=1, tiled=True)  38 us
    ppermute x16, starting transfers between devices, hypercube_sum(): value = value + lax.ppermute(value, axis, pairs)  32.8 us
    another operation x15, other arithmetic, inverse_factor(): factor = jnp.linalg.cholesky(gram_block)  32.7 us
    another operation x10, other arithmetic, inverse_factor(): return jax.scipy.linalg.solve_triangular(factor, identity, lower=True)  27.7 us
  transfers between devices with their start and end apart: 20, of which 17 were waited for; matrix products, arithmetic and copies ran while one was open for 17% of the time, Pallas kernels for 0%

profile of v3, /device:TPU:8, one launch (start us, length us, event | category | flops | bytes accessed | tf_op | source)
XLA Modules:
  0.0 410.9 jit_solution(6654950625014713800)
XLA Ops:
  7.2 0.7 all-gather.3.cloned.1.call-update
  7.9 0.7 all-gather.5.cloned.1.call-update
  8.7 1.2 pad_maximum_fusion
  11.1 1.9 collective-permute-done
  13.0 2.0 collective-permute-start.1
  15.0 12.6 %collective-permute-done.1 = f32[15,64,64]{1,2,0:T(8,128)S(1)} collective-permute-done((f32[15,64,64]{1,2,0:T(8,128)S(1)}, f32[15,64,64]{1,2,0:T(8,128)S(1)}, u32[]{:S(2)}, u32[]{:S(2)}) %collective-permute-start.1) | collective-permute-done | bytes 245792 | tf_op jit(solution)/shard_map/ppermute | solution.py:61
  27.7 3.8 collective-permute-start.2
  31.5 28.9 %collective-permute-done.2 = f32[15,64,64]{1,2,0:T(8,128)S(1)} collective-permute-done((f32[15,64,64]{1,2,0:T(8,128)S(1)}, f32[15,64,64]{1,2,0:T(8,128)S(1)}, u32[]{:S(2)}, u32[]{:S(2)}) %collective-permute-start.2) | collective-permute-done | bytes 245792 | tf_op jit(solution)/shard_map/ppermute | solution.py:61
  60.4 5.5 %collective-permute-start.3 = (f32[15,64,64]{1,2,0:T(8,128)S(1)}, f32[15,64,64]{1,2,0:T(8,128)S(1)}, u32[]{:S(2)}, u32[]{:S(2)}) collective-permute-start(f32[15,64,64]{1,2,0:T(8,128)S(1)} %add.182), channel_id=1, source_target_pairs={{0,8},{1,9},{2,10},{3,11},{4,12},{5,13},{6,14},{7,15},{8,0},{9,1},... | collective-permute-start | bytes 737288 | tf_op jit(solution)/shard_map/ppermute | solution.py:61
  65.9 21.7 %collective-permute-done.3 = f32[15,64,64]{1,2,0:T(8,128)S(1)} collective-permute-done((f32[15,64,64]{1,2,0:T(8,128)S(1)}, f32[15,64,64]{1,2,0:T(8,128)S(1)}, u32[]{:S(2)}, u32[]{:S(2)}) %collective-permute-start.3) | collective-permute-done | bytes 245792 | tf_op jit(solution)/shard_map/ppermute | solution.py:61
  87.7 1.6 collective-permute-start.4
  89.3 8.7 %collective-permute-done.4 = f32[15,64,64]{1,2,0:T(8,128)S(1)} collective-permute-done((f32[15,64,64]{1,2,0:T(8,128)S(1)}, f32[15,64,64]{1,2,0:T(8,128)S(1)}, u32[]{:S(2)}, u32[]{:S(2)}) %collective-permute-start.4) | collective-permute-done | bytes 245792 | tf_op jit(solution)/shard_map/ppermute | solution.py:61
  98.0 3.1 collective-permute-start.5
  101.2 17.7 %collective-permute-done.5 = f32[15,64,64]{1,2,0:T(8,128)S(1)} collective-permute-done((f32[15,64,64]{1,2,0:T(8,128)S(1)}, f32[15,64,64]{1,2,0:T(8,128)S(1)}, u32[]{:S(2)}, u32[]{:S(2)}) %collective-permute-start.5) | collective-permute-done | bytes 245792 | tf_op jit(solution)/shard_map/ppermute | solution.py:61
  119.0 0.8 collective-permute-start.6
  119.8 0.7 fusion.111
  141.6 2.0 collective-permute-start.7
  143.6 5.7 %slice_bitcast_fusion = (bf16[1024,1024]{1,0:T(8,128)(2,1)S(1)}, bf16[1024,1024]{1,0:T(8,128)(2,1)}, bf16[1024,1024]{1,0:T(8,128)(2,1)}, bf16[1024,1024]{1,0:T(8,128)(2,1)}) fusion(bf16[5,1024,1024]{2,1,0:T(8,128)(2,1)} %param.21), kind=kLoop, calls=%fused_computation.38 | loop fusion | bytes 16777216 | tf_op jit(solution)/shard_map/squeeze | solution.py:24
  149.3 2.7 collective-permute-done.7
  152.1 12.9 %conditional.5 = (f32[64,16384]{1,0:T(8,128)}, f32[64,16384]{1,0:T(8,128)}) conditional(s32[]{:T(128)} %bitcast.6, () %tuple.51, (s32[]{:T(128)}, bf16[64,16384]{1,0:T(8,128)(2,1)}, bf16[1024,1024]{1,0:T(8,128)(2,1)}, s32[]{:T(128)}, bf16[64,16384]{1,0:T(8,128)(2,1)}) %tuple.53), branch_computations={%region_0.1_spmd, %region_1.2_spmd} | conditional | flops 268435456 | bytes 14418028 | solution.py:40
  152.1 2.4 fusion.2
  154.6 2.3 broadcast.52.clone
  156.9 1.8 dynamic_update_slice.26
  158.7 2.2 fusion
  160.9 2.3 broadcast.52.clone.1
  163.2 1.8 dynamic_update_slice.27
  166.1 5.8 %cholesky.89 = f32[64,64]{1,0:T(8,128)S(1)} custom-call(f32[64,64]{1,0:T(8,128)S(1)} %get-tuple-element.357), custom_call_target="Cholesky" | custom-call | tf_op jit(solution)/shard_map/jit(cholesky)/cholesky | solution.py:67
  172.0 0.6 compare_reduce_fusion.4
  172.6 0.7 fusion.50
  173.3 4.9 %custom-call.9 = f32[1,64,64]{1,2,0:T(8,128)S(1)} custom-call(f32[1,64,64]{2,1,0:T(8,128)S(1)} %fusion.50), custom_call_target="InvertDiagBlocksLowerTriangular" | custom-call | tf_op jit(solution)/shard_map/jit(_solve_triangular)/triangular_solve | solution.py:69
  178.2 5.9 %cholesky.100 = f32[64,64]{1,0:T(8,128)S(1)} custom-call(f32[64,64]{1,0:T(8,128)S(1)} %get-tuple-element.358), custom_call_target="Cholesky" | custom-call | tf_op jit(solution)/shard_map/jit(cholesky)/cholesky | solution.py:67
  184.1 0.6 compare_reduce_fusion.3
  184.7 0.7 fusion.51
  185.4 4.9 %custom-call.10 = f32[1,64,64]{1,2,0:T(8,128)S(1)} custom-call(f32[1,64,64]{2,1,0:T(8,128)S(1)} %fusion.51), custom_call_target="InvertDiagBlocksLowerTriangular" | custom-call | tf_op jit(solution)/shard_map/jit(_solve_triangular)/triangular_solve | solution.py:69
  190.3 5.9 %cholesky.111 = f32[64,64]{1,0:T(8,128)S(1)} custom-call(f32[64,64]{1,0:T(8,128)S(1)} %get-tuple-element.359), custom_call_target="Cholesky" | custom-call | tf_op jit(solution)/shard_map/jit(cholesky)/cholesky | solution.py:67
  196.2 0.6 compare_reduce_fusion.2
  196.8 0.7 fusion.52
  197.5 4.9 %custom-call.11 = f32[1,64,64]{1,2,0:T(8,128)S(1)} custom-call(f32[1,64,64]{2,1,0:T(8,128)S(1)} %fusion.52), custom_call_target="InvertDiagBlocksLowerTriangular" | custom-call | tf_op jit(solution)/shard_map/jit(_solve_triangular)/triangular_solve | solution.py:69
  202.4 5.9 %cholesky.122 = f32[64,64]{1,0:T(8,128)S(1)} custom-call(f32[64,64]{1,0:T(8,128)S(1)} %get-tuple-element.360), custom_call_target="Cholesky" | custom-call | tf_op jit(solution)/shard_map/jit(cholesky)/cholesky | solution.py:67
  208.3 0.6 compare_reduce_fusion.1
  208.9 0.7 fusion.53
  209.6 4.9 %custom-call.12 = f32[1,64,64]{1,2,0:T(8,128)S(1)} custom-call(f32[1,64,64]{2,1,0:T(8,128)S(1)} %fusion.53), custom_call_target="InvertDiagBlocksLowerTriangular" | custom-call | tf_op jit(solution)/shard_map/jit(_solve_triangular)/triangular_solve | solution.py:69
  214.5 5.9 %cholesky.133 = f32[64,64]{1,0:T(8,128)S(1)} custom-call(f32[64,64]{1,0:T(8,128)S(1)} %get-tuple-element.356), custom_call_target="Cholesky" | custom-call | tf_op jit(solution)/shard_map/jit(cholesky)/cholesky | solution.py:67
  220.4 0.6 compare_reduce_fusion
  221.0 0.7 fusion.54
  221.7 4.9 %custom-call.13 = f32[1,64,64]{1,2,0:T(8,128)S(1)} custom-call(f32[1,64,64]{2,1,0:T(8,128)S(1)} %fusion.54), custom_call_target="InvertDiagBlocksLowerTriangular" | custom-call | tf_op jit(solution)/shard_map/jit(_solve_triangular)/triangular_solve | solution.py:69
  227.8 38.0 %reduce-scatter.3.cloned.1.call-done = f32[64,1024]{1,0:T(8,128)} async-done(((f32[64,16384]{1,0:T(8,128)}), f32[64,1024]{1,0:T(8,128)}) %reduce-scatter.3.cloned.1.call-update) | async-done | bytes 262160 | tf_op jit(solution)/shard_map/reduce_scatter | solution.py:45
  265.8 84.6 %reduce-scatter.5.cloned.1.call-done = f32[64,1024]{1,0:T(8,128)} async-done(((f32[64,16384]{1,0:T(8,128)}), f32[64,1024]{1,0:T(8,128)}) %reduce-scatter.5.cloned.1.call-update) | async-done | bytes 262160 | tf_op jit(solution)/shard_map/reduce_scatter | solution.py:49
  350.4 1.8 fusion.110
  352.3 1.3 collective-permute-done.8
  353.6 1.6 collective-permute-start.9
  355.2 3.3 collective-permute-done.9
  358.5 2.6 collective-permute-start.10
  361.1 4.5 %collective-permute-done.10 = f32[320,64]{0,1:T(8,128)S(1)} collective-permute-done((f32[320,64]{0,1:T(8,128)S(1)}, f32[320,64]{0,1:T(8,128)S(1)}, u32[]{:S(2)}, u32[]{:S(2)}) %collective-permute-start.10) | collective-permute-done | bytes 81952 | tf_op jit(solution)/shard_map/ppermute | solution.py:61
  365.7 6.0 %collective-permute-start.11 = (f32[320,64]{0,1:T(8,128)S(1)}, f32[320,64]{0,1:T(8,128)S(1)}, u32[]{:S(2)}, u32[]{:S(2)}) collective-permute-start(f32[320,64]{0,1:T(8,128)S(1)} %add.196), channel_id=1, source_target_pairs={{0,8},{1,9},{2,10},{3,11},{4,12},{5,13},{6,14},{7,15},{8,0},{9,1},... | collective-permute-start | bytes 245768 | tf_op jit(solution)/shard_map/ppermute | solution.py:61
  371.7 3.8 collective-permute-done.11
  376.0 5.1 %collective-permute-done.12 = f32[320,64]{0,1:T(8,128)S(1)} collective-permute-done((f32[320,64]{0,1:T(8,128)S(1)}, f32[320,64]{0,1:T(8,128)S(1)}, u32[]{:S(2)}, u32[]{:S(2)}) %collective-permute-start.12) | collective-permute-done | bytes 81952 | tf_op jit(solution)/shard_map/ppermute | solution.py:61
  381.1 0.8 collective-permute-start.13
  381.9 5.4 %collective-permute-done.13 = f32[320,64]{0,1:T(8,128)S(1)} collective-permute-done((f32[320,64]{0,1:T(8,128)S(1)}, f32[320,64]{0,1:T(8,128)S(1)}, u32[]{:S(2)}, u32[]{:S(2)}) %collective-permute-start.13) | collective-permute-done | bytes 81952 | tf_op jit(solution)/shard_map/ppermute | solution.py:61
  387.5 4.6 %collective-permute-done.14 = f32[320,64]{0,1:T(8,128)S(1)} collective-permute-done((f32[320,64]{0,1:T(8,128)S(1)}, f32[320,64]{0,1:T(8,128)S(1)}, u32[]{:S(2)}, u32[]{:S(2)}) %collective-permute-start.14) | collective-permute-done | bytes 81952 | tf_op jit(solution)/shard_map/ppermute | solution.py:61
  392.0 2.2 collective-permute-start.15
  394.2 4.0 collective-permute-done.15
  402.4 1.2 convolution_subtract_fusion
  403.6 0.8 copy.27
  (97 shorter events, 8.8 us)
Async XLA Ops:
  7.2 144.9 %all-gather.3.cloned.1.call-start = ((), (), s32[]{:S(2)}) async-start(), calls=%async_computation.2 | async-start | bytes 2228224 | tf_op jit(solution)/shard_map/all_gather | solution.py:86
  7.9 144.2 %all-gather.5.cloned.1.call-start = ((), (), s32[]{:S(2)}) async-start(), calls=%async_computation.3 | async-start | bytes 2228224 | tf_op jit(solution)/shard_map/all_gather | solution.py:87
  8.6 257.2 %reduce-scatter.3.cloned.1.call-start = ((), (), s32[]{:S(2)}) async-start(), calls=%async_computation.4 | async-start | bytes 4456448 | tf_op jit(solution)/shard_map/reduce_scatter | solution.py:45
  11.0 2.0 collective-permute-start
  13.0 14.6 %collective-permute-start.1 = (f32[15,64,64]{1,2,0:T(8,128)S(1)}, f32[15,64,64]{1,2,0:T(8,128)S(1)}, u32[]{:S(2)}, u32[]{:S(2)}) collective-permute-start(f32[15,64,64]{1,2,0:T(8,128)S(1)} %add.180), channel_id=1, source_target_pairs={{0,2},{1,3},{2,0},{3,1},{4,6},{5,7},{6,4},{7,5},{8,10},{9,11},{10,... | collective-permute-start | bytes 737288 | tf_op jit(solution)/shard_map/ppermute | solution.py:61
  27.7 32.7 %collective-permute-start.2 = (f32[15,64,64]{1,2,0:T(8,128)S(1)}, f32[15,64,64]{1,2,0:T(8,128)S(1)}, u32[]{:S(2)}, u32[]{:S(2)}) collective-permute-start(f32[15,64,64]{1,2,0:T(8,128)S(1)} %add.181), channel_id=1, source_target_pairs={{0,4},{1,5},{2,6},{3,7},{4,0},{5,1},{6,2},{7,3},{8,12},{9,13},{10,... | collective-permute-start | bytes 737288 | tf_op jit(solution)/shard_map/ppermute | solution.py:61
  60.4 59.4 %copy-start.3 = (s32[5,3]{0,1:T(4,128)S(1)}, s32[5,3]{0,1:T(4,128)}, u32[]{:S(2)}) copy-start(s32[5,3]{0,1:T(4,128)} %param.22) | copy-start | bytes 184
  60.4 27.2 %collective-permute-start.3 = (f32[15,64,64]{1,2,0:T(8,128)S(1)}, f32[15,64,64]{1,2,0:T(8,128)S(1)}, u32[]{:S(2)}, u32[]{:S(2)}) collective-permute-start(f32[15,64,64]{1,2,0:T(8,128)S(1)} %add.182), channel_id=1, source_target_pairs={{0,8},{1,9},{2,10},{3,11},{4,12},{5,13},{6,14},{7,15},{8,0},{9,1},... | collective-permute-start | bytes 737288 | tf_op jit(solution)/shard_map/ppermute | solution.py:61
  87.7 10.3 %collective-permute-start.4 = (f32[15,64,64]{1,2,0:T(8,128)S(1)}, f32[15,64,64]{1,2,0:T(8,128)S(1)}, u32[]{:S(2)}, u32[]{:S(2)}) collective-permute-start(f32[15,64,64]{1,2,0:T(8,128)S(1)} %add.183), channel_id=1, source_target_pairs={{0,16},{16,0},{32,48},{48,32},{64,80},{80,64},{96,112},{112,96},{1... | collective-permute-start | bytes 737288 | tf_op jit(solution)/shard_map/ppermute | solution.py:61
  98.0 20.9 %collective-permute-start.5 = (f32[15,64,64]{1,2,0:T(8,128)S(1)}, f32[15,64,64]{1,2,0:T(8,128)S(1)}, u32[]{:S(2)}, u32[]{:S(2)}) collective-permute-start(f32[15,64,64]{1,2,0:T(8,128)S(1)} %add.184), channel_id=1, source_target_pairs={{0,32},{16,48},{32,0},{48,16},{64,96},{80,112},{96,64},{112,80},{1... | collective-permute-start | bytes 737288 | tf_op jit(solution)/shard_map/ppermute | solution.py:61
  119.0 22.5 %collective-permute-start.6 = (f32[15,64,64]{1,2,0:T(8,128)S(1)}, f32[15,64,64]{1,2,0:T(8,128)S(1)}, u32[]{:S(2)}, u32[]{:S(2)}) collective-permute-start(f32[15,64,64]{1,2,0:T(8,128)S(1)} %add.185), channel_id=1, source_target_pairs={{0,64},{16,80},{32,96},{48,112},{64,0},{80,16},{96,32},{112,48},{1... | collective-permute-start | bytes 737288 | tf_op jit(solution)/shard_map/ppermute | solution.py:61
  141.6 10.4 %collective-permute-start.7 = (f32[15,64,64]{1,2,0:T(8,128)S(1)}, f32[15,64,64]{1,2,0:T(8,128)S(1)}, u32[]{:S(2)}, u32[]{:S(2)}) collective-permute-start(f32[15,64,64]{1,2,0:T(8,128)S(1)} %add.186), channel_id=1, source_target_pairs={{0,128},{16,144},{32,160},{48,176},{64,192},{80,208},{96,224},{112... | collective-permute-start | bytes 737288 | tf_op jit(solution)/shard_map/ppermute | solution.py:61
  165.0 185.4 %reduce-scatter.5.cloned.1.call-start = ((), (), s32[]{:S(2)}) async-start(), calls=%async_computation.5 | async-start | bytes 4456448 | tf_op jit(solution)/shard_map/reduce_scatter | solution.py:49
  165.3 185.1 %copy-start = (bf16[64,1024]{1,0:T(8,128)(2,1)S(1)}, bf16[64,1024]{1,0:T(8,128)(2,1)}, u32[]{:S(2)}) copy-start(bf16[64,1024]{1,0:T(8,128)(2,1)} %param.18) | copy-start | bytes 393220
  165.3 185.1 %copy-start.4 = (f32[1024]{0:T(1024)S(1)}, f32[1024]{0:T(1024)}, u32[]{:S(2)}) copy-start(f32[1024]{0:T(1024)} %param.20) | copy-start | bytes 12292
  352.2 1.4 collective-permute-start.8
  353.6 4.9 %collective-permute-start.9 = (f32[320,64]{0,1:T(8,128)S(1)}, f32[320,64]{0,1:T(8,128)S(1)}, u32[]{:S(2)}, u32[]{:S(2)}) collective-permute-start(f32[320,64]{0,1:T(8,128)S(1)} %add.194), channel_id=1, source_target_pairs={{0,2},{1,3},{2,0},{3,1},{4,6},{5,7},{6,4},{7,5},{8,10},{9,11},{10,... | collective-permute-start | bytes 245768 | tf_op jit(solution)/shard_map/ppermute | solution.py:61
  358.5 7.1 %collective-permute-start.10 = (f32[320,64]{0,1:T(8,128)S(1)}, f32[320,64]{0,1:T(8,128)S(1)}, u32[]{:S(2)}, u32[]{:S(2)}) collective-permute-start(f32[320,64]{0,1:T(8,128)S(1)} %add.195), channel_id=1, source_target_pairs={{0,4},{1,5},{2,6},{3,7},{4,0},{5,1},{6,2},{7,3},{8,12},{9,13},{10,... | collective-permute-start | bytes 245768 | tf_op jit(solution)/shard_map/ppermute | solution.py:61
  365.7 36.7 %copy-start.1 = (f32[64,1024]{1,0:T(8,128)S(1)}, f32[64,1024]{1,0:T(8,128)}, u32[]{:S(2)}) copy-start(f32[64,1024]{1,0:T(8,128)} %reduce-scatter.3.cloned.1.call-done) | copy-start | bytes 786436
  365.7 36.7 %copy-start.2 = (f32[64,1024]{1,0:T(8,128)S(1)}, f32[64,1024]{1,0:T(8,128)}, u32[]{:S(2)}) copy-start(f32[64,1024]{1,0:T(8,128)} %reduce-scatter.5.cloned.1.call-done) | copy-start | bytes 786436
  365.7 9.9 %collective-permute-start.11 = (f32[320,64]{0,1:T(8,128)S(1)}, f32[320,64]{0,1:T(8,128)S(1)}, u32[]{:S(2)}, u32[]{:S(2)}) collective-permute-start(f32[320,64]{0,1:T(8,128)S(1)} %add.196), channel_id=1, source_target_pairs={{0,8},{1,9},{2,10},{3,11},{4,12},{5,13},{6,14},{7,15},{8,0},{9,1},... | collective-permute-start | bytes 245768 | tf_op jit(solution)/shard_map/ppermute | solution.py:61
  375.6 5.5 %collective-permute-start.12 = (f32[320,64]{0,1:T(8,128)S(1)}, f32[320,64]{0,1:T(8,128)S(1)}, u32[]{:S(2)}, u32[]{:S(2)}) collective-permute-start(f32[320,64]{0,1:T(8,128)S(1)} %add.197), channel_id=1, source_target_pairs={{0,16},{16,0},{32,48},{48,32},{64,80},{80,64},{96,112},{112,96},{1... | collective-permute-start | bytes 245768 | tf_op jit(solution)/shard_map/ppermute | solution.py:61
  381.1 6.2 %collective-permute-start.13 = (f32[320,64]{0,1:T(8,128)S(1)}, f32[320,64]{0,1:T(8,128)S(1)}, u32[]{:S(2)}, u32[]{:S(2)}) collective-permute-start(f32[320,64]{0,1:T(8,128)S(1)} %add.198), channel_id=1, source_target_pairs={{0,32},{16,48},{32,0},{48,16},{64,96},{80,112},{96,64},{112,80},{1... | collective-permute-start | bytes 245768 | tf_op jit(solution)/shard_map/ppermute | solution.py:61
  387.3 4.7 %collective-permute-start.14 = (f32[320,64]{0,1:T(8,128)S(1)}, f32[320,64]{0,1:T(8,128)S(1)}, u32[]{:S(2)}, u32[]{:S(2)}) collective-permute-start(f32[320,64]{0,1:T(8,128)S(1)} %add.199), channel_id=1, source_target_pairs={{0,64},{16,80},{32,96},{48,112},{64,0},{80,16},{96,32},{112,48},{1... | collective-permute-start | bytes 245768 | tf_op jit(solution)/shard_map/ppermute | solution.py:61
  392.0 6.2 %collective-permute-start.15 = (f32[320,64]{0,1:T(8,128)S(1)}, f32[320,64]{0,1:T(8,128)S(1)}, u32[]{:S(2)}, u32[]{:S(2)}) collective-permute-start(f32[320,64]{0,1:T(8,128)S(1)} %add.200), channel_id=1, source_target_pairs={{0,128},{16,144},{32,160},{48,176},{64,192},{80,208},{96,224},{112... | collective-permute-start | bytes 245768 | tf_op jit(solution)/shard_map/ppermute | solution.py:61
Sparse Core Ops, SparseCore 0:
  9.8 52.0 all-gather.2
  64.4 53.8 all-gather.4
  165.2 100.6 reduce-scatter.2
  269.3 81.0 reduce-scatter.4
